TPU v7x, 32 devices: a whole 2x2x4 slice. The times are simulated.
32 devices in a mesh: blk: 4 (over y, x), group: 8 (over z, core).
Axes of the slice: x: 2, y: 2, z: 4, core: 2. Of those that a mesh axis runs over, the one named last changes fastest.
Arguments:
- picture_vector_list: bfloat16 [8, 1024, 768], P('group', 'blk'), may hold values from -0.25 to 0.25
- caption_latent_matrix: bfloat16 [8, 1024, 3072], P('group', 'blk'), may hold values from -6 to 6
- linear_map_matrix: bfloat16 [3072, 768], P('group'), may hold values from -0.109375 to 0.109375
- target_match_index: int32 [8, 1024], P('group', 'blk'), may hold values from 0 to 1023, each once within a row
- sharpness_factor: float32 [1], replicated, may hold values from 24 to 40
- offset_term: float32 [1], replicated, may hold values from -6 to -5
Outputs:
- row_loss: float32 [8, 1024], P('group', 'blk')
- image_grad: bfloat16 [8, 1024, 768], P('group', 'blk')
- projection_grad: float32 [3072, 768], P(('blk', 'group'))
Inputs may be any that keep to these rules, and one draw needn't show every extreme that they name: `target_match_index`: each data group's row of positives is a permutation of 0 to 1023.
All inputs are finite; a program needn't handle non-finite values.
Results may differ from a plain program's by a relative error of at most 0.015.
Values may be sent and summed in bfloat16 or wider, within the bound.
No kernel may reach another device: no remote copies, remote signals or barrier semaphores. Data moves between devices by JAX's collectives and lax.ppermute only.
A program may use at most 64 MiB of HBM per device.

v0:
```python
import jax
import jax.numpy as jnp
from jax import lax
from jax.sharding import PartitionSpec as P

epsilon = 1e-06


def passed_along(value, axis, steps):
    count = lax.axis_size(axis)
    pairs = [(source, (source + steps) % count) for source in range(count)]
    return lax.ppermute(value, axis, pairs)


def body(
    picture_vector_list,
    caption_latent_matrix,
    linear_map_matrix,
    target_match_index,
    sharpness_factor,
    offset_term,
):
    image_rows = picture_vector_list[0]
    hidden_rows = caption_latent_matrix[0]
    label_rows = target_match_index[0]
    row_count = image_rows.shape[0]
    feature_dim = image_rows.shape[1]
    blocks = lax.axis_size("blk")
    my_index = lax.axis_index("blk")
    multiplier_amount = sharpness_factor[0]
    offset_value = offset_term[0]
    columns = hidden_rows
    projected = jnp.dot(
        columns,
        lax.all_gather(linear_map_matrix, "group", axis=0, tiled=True),
        preferred_element_type=jnp.float32,
    )
    text_scale = lax.rsqrt(jnp.sum(projected * projected, axis=1, keepdims=True) + epsilon)
    text_dir = projected * text_scale
    text_unit = text_dir.astype(jnp.bfloat16)
    image_float = image_rows.astype(jnp.float32)
    image_scale = lax.rsqrt(jnp.sum(image_float * image_float, axis=1, keepdims=True) + epsilon)
    image_dir = image_float * image_scale
    image_unit = image_dir.astype(jnp.bfloat16)

    def signed_logits(image_tile_rows, label_block, text_block, column_start):
        columns = column_start + jnp.arange(text_block.shape[0], dtype=jnp.int32)
        pair_sign = jnp.where(label_block[:, None] == columns[None, :], 1.0, -1.0).astype(
            jnp.float32
        )
        pair_scores = lax.dot_general(
            image_tile_rows,
            text_block,
            (((1,), (1,)), ((), ())),
            preferred_element_type=jnp.float32,
        )
        return (multiplier_amount * pair_scores + offset_value, pair_sign)

    def weights_of(logits, pair_sign):
        return (-pair_sign * jax.nn.sigmoid(-pair_sign * logits) * multiplier_amount).astype(
            jnp.bfloat16
        )

    image_unit_grad = jnp.zeros((row_count, feature_dim), jnp.float32)
    loss_local = jnp.zeros((row_count,), jnp.float32)
    text_block = text_unit
    for step_index in range(blocks):
        source = (my_index - step_index) % blocks
        logits, pair_sign = signed_logits(image_unit, label_rows, text_block, source * row_count)
        loss_local = loss_local + -jnp.sum(jax.nn.log_sigmoid(pair_sign * logits), axis=1)
        pair_weight = weights_of(logits, pair_sign)
        image_unit_grad = image_unit_grad + jnp.dot(
            pair_weight, text_block, preferred_element_type=jnp.float32
        )
        if step_index + 1 < blocks:
            text_block = passed_along(text_block, "blk", 1)
    own_start = my_index * row_count
    image_piece = lax.all_gather(image_unit, "blk", axis=0, tiled=True)
    label_piece = lax.all_gather(label_rows, "blk", axis=0, tiled=True)
    logits, pair_sign = signed_logits(image_piece, label_piece, text_unit, own_start)
    pair_weight = weights_of(logits, pair_sign)
    text_unit_grad = lax.dot_general(
        pair_weight, image_piece, (((0,), (0,)), ((), ())), preferred_element_type=jnp.float32
    )
    image_grad = (
        image_scale
        * (
            image_unit_grad
            - image_dir * jnp.sum(image_dir * image_unit_grad, axis=1, keepdims=True)
        )
    ).astype(jnp.bfloat16)
    projection_output_gradient = (
        text_scale
        * (text_unit_grad - text_dir * jnp.sum(text_dir * text_unit_grad, axis=1, keepdims=True))
    ).astype(jnp.bfloat16)
    columns = hidden_rows
    projection_grad = lax.psum_scatter(
        lax.dot_general(
            columns,
            projection_output_gradient,
            (((0,), (0,)), ((), ())),
            preferred_element_type=jnp.float32,
        ),
        ("blk", "group"),
        scatter_dimension=0,
        tiled=True,
    )
    return (loss_local[None], image_grad[None], projection_grad)


def solution(mesh):
    return jax.shard_map(
        body,
        mesh=mesh,
        in_specs=(
            P("group", "blk", None),
            P("group", "blk", None),
            P("group", None),
            P("group", "blk"),
            P(),
            P(),
        ),
        out_specs=(P("group", "blk"), P("group", "blk", None), P(("blk", "group"), None)),
        check_vma=False,
    )
```

profile of v0, /device:TPU:0, one launch (start us, length us, event | category | flops | bytes accessed | tf_op | source)
XLA Modules:
  0.0 257.5 jit_solution(9647050227928517033)
XLA Ops:
  7.2 0.7 all-gather.4.cloned.1.call-update
  8.0 1.2 fusion.27
  9.1 1.9 fusion.22
  12.4 10.1 %all-gather = s32[1,1024]{1,0:T(1,128)} all-gather(s32[1,256]{1,0:T(1,128)S(1)} %copy-done.3), channel_id=2, replica_groups=mesh['blk'=4,'group'=8] {'blk'}, dimensions={1}, use_global_device_ids=true | all-gather | bytes 5120 | tf_op jit(solution)/shard_map/all_gather | solution.py:79
  22.5 0.6 iota_add_fusion
  23.0 41.1 %all-gather.4.cloned.1.call-done = bf16[3072,768]{1,0:T(8,128)(2,1)} async-done(((bf16[384,768]{1,0:T(8,128)(2,1)}), bf16[3072,768]{1,0:T(8,128)(2,1)}) %all-gather.4.cloned.1.call-update) | async-done | bytes 4718608 | tf_op jit(solution)/shard_map/all_gather | solution.py:35
  64.1 3.8 %multiply_reduce_fusion.1 = (f32[256]{0:T(256)S(1)}, f32[256,768]{1,0:T(8,128)S(1)}) fusion(bf16[3072,768]{1,0:T(8,128)(2,1)} %all-gather.4.cloned.1.call-done, bf16[1,256,3072]{2,1,0:T(8,128)(2,1)S(1)} %copy-done), kind=kOutput, calls=%fused_computation.41 | convolution fusion | flops 1208352512 | bytes 7078912 | tf_op jit(solution)/shard_map/dot_general | solution.py:33
  68.0 28.3 %all-gather.6.cloned.1.call-done = bf16[1024,768]{1,0:T(8,128)(2,1)} async-done(((bf16[256,768]{1,0:T(8,128)(2,1)}), bf16[1024,768]{1,0:T(8,128)(2,1)}) %all-gather.6.cloned.1.call-update) | async-done | bytes 1572880 | tf_op jit(solution)/shard_map/all_gather | solution.py:78
  96.3 3.9 %multiply_reduce_fusion = (f32[256]{0:T(256)S(1)}, f32[256,768]{1,0:T(8,128)S(1)}) fusion(f32[256,768]{1,0:T(8,128)S(1)} %get-tuple-element.14, f32[256]{0:T(256)S(1)} %add_rsqrt_fusion, bf16[1024,768]{1,0:T(8,128)(2,1)} %all-gather.6.cloned.1.call-done, bf16[256,768]{1,0:T(8,128)(2,1)S(1)} %multiply_convert_fusion.1, f32[]{:T(128)} %bitcast.49, ...), kind=kOutput, calls=%fused_computation.40 | convolution fusion | flops 809041664 | bytes 3546120 | tf_op jit(solution)/shard_map/dot_general | solution.py:82
  100.2 5.3 %convolution_bitcast_fusion = f32[3072,768]{0,1:T(8,128)} fusion(bf16[1,256,3072]{2,1,0:T(8,128)(2,1)S(1)} %copy-done, f32[256,768]{1,0:T(8,128)S(1)} %get-tuple-element.19, f32[256,768]{1,0:T(8,128)S(1)} %get-tuple-element.14, f32[256]{0:T(256)S(1)} %get-tuple-element.18, f32[256]{0:T(256)S(1)} %add_rsqrt_fusion), kind=kOutput, calls=%fused_computation | convolution fusion | flops 1208942592 | bytes 12584960 | tf_op jit(solution)/shard_map/dot_general | solution.py:98
  105.5 9.6 %copy.11 = f32[3072,768]{1,0:T(8,128)} copy(f32[3072,768]{0,1:T(8,128)} %convolution_bitcast_fusion) | data formatting | bytes 18874368
  115.2 1.5 collective-permute-start
  116.7 10.3 %collective-permute-done = bf16[256,768]{1,0:T(8,128)(2,1)S(1)} collective-permute-done((bf16[256,768]{1,0:T(8,128)(2,1)S(1)}, bf16[256,768]{1,0:T(8,128)(2,1)S(1)}, u32[]{:S(2)}, u32[]{:S(2)}) %collective-permute-start) | collective-permute-done | bytes 393248 | tf_op jit(solution)/shard_map/ppermute | solution.py:12
  127.0 0.6 collective-permute-start.1
  127.8 10.0 %collective-permute-done.1 = bf16[256,768]{1,0:T(8,128)(2,1)S(1)} collective-permute-done((bf16[256,768]{1,0:T(8,128)(2,1)S(1)}, bf16[256,768]{1,0:T(8,128)(2,1)S(1)}, u32[]{:S(2)}, u32[]{:S(2)}) %collective-permute-start.1) | collective-permute-done | bytes 393248 | tf_op jit(solution)/shard_map/ppermute | solution.py:12
  137.8 0.4 fusion.77
  138.6 9.2 %collective-permute-done.2 = bf16[256,768]{1,0:T(8,128)(2,1)S(1)} collective-permute-done((bf16[256,768]{1,0:T(8,128)(2,1)S(1)}, bf16[256,768]{1,0:T(8,128)(2,1)S(1)}, u32[]{:S(2)}, u32[]{:S(2)}) %collective-permute-start.2) | collective-permute-done | bytes 393248 | tf_op jit(solution)/shard_map/ppermute | solution.py:12
  148.1 0.9 fusion.70
  149.0 0.6 add_add_fusion
  150.0 0.4 convolution_add_fusion.1
  150.5 0.5 copy-done.2
  151.0 0.5 fusion.23
  151.6 1.0 fusion.34
  152.5 98.5 %reduce-scatter.4.cloned.1.call-done = f32[96,768]{1,0:T(8,128)} async-done(((f32[3072,768]{1,0:T(8,128)}), f32[96,768]{1,0:T(8,128)}) %reduce-scatter.4.cloned.1.call-update) | async-done | bytes 294928
  (22 shorter events, 1.7 us)
Async XLA Ops:
  7.2 56.9 %copy-start = (bf16[1,256,3072]{2,1,0:T(8,128)(2,1)S(1)}, bf16[1,256,3072]{2,1,0:T(8,128)(2,1)}, u32[]{:S(2)}) copy-start(bf16[1,256,3072]{2,1,0:T(8,128)(2,1)} %param.7) | copy-start | bytes 4718596
  7.2 5.2 %copy-start.3 = (s32[1,256]{1,0:T(1,128)S(1)}, s32[1,256]{1,0:T(1,128)}, u32[]{:S(2)}) copy-start(s32[1,256]{1,0:T(1,128)} %param.9) | copy-start | bytes 3076
  7.2 56.9 %all-gather.4.cloned.1.call-start = ((), (), s32[]{:S(2)}) async-start(), calls=%async_computation.1 | async-start | bytes 5308416 | tf_op jit(solution)/shard_map/all_gather | solution.py:35
  7.9 88.4 %all-gather.6.cloned.1.call-start = ((), (), s32[]{:S(2)}) async-start(), calls=%async_computation.2 | async-start | bytes 1966080 | tf_op jit(solution)/shard_map/all_gather | solution.py:78
  11.0 240.0 %reduce-scatter.4.cloned.1.call-start = ((), (), s32[]{:S(2)}) async-start(), calls=%async_computation.3 | async-start | bytes 9732096
  115.1 12.4 %copy-start.1 = (bf16[256,768]{1,0:T(8,128)(2,1)S(1)}, bf16[256,768]{1,0:T(8,128)(2,1)}, u32[]{:S(2)}) copy-start(bf16[256,768]{1,0:T(8,128)(2,1)} %fusion.22) | copy-start | bytes 1179652
  115.2 11.8 %collective-permute-start = (bf16[256,768]{1,0:T(8,128)(2,1)S(1)}, bf16[256,768]{1,0:T(8,128)(2,1)S(1)}, u32[]{:S(2)}, u32[]{:S(2)}) collective-permute-start(bf16[256,768]{1,0:T(8,128)(2,1)S(1)} %multiply_convert_fusion.1), channel_id=1, source_target_pairs={{0,8},{8,16},{16,24},{24,0},{1,9},{9,17},{17,25},{25,1},{2,10},{10... | collective-permute-start | bytes 1179656 | tf_op jit(solution)/shard_map/ppermute | solution.py:12
  127.0 10.9 %collective-permute-start.1 = (bf16[256,768]{1,0:T(8,128)(2,1)S(1)}, bf16[256,768]{1,0:T(8,128)(2,1)S(1)}, u32[]{:S(2)}, u32[]{:S(2)}) collective-permute-start(bf16[256,768]{1,0:T(8,128)(2,1)S(1)} %collective-permute-done), channel_id=1, source_target_pairs={{0,8},{8,16},{16,24},{24,0},{1,9},{9,17},{17,25},{25,1},{2,10},{10... | collective-permute-start | bytes 1179656 | tf_op jit(solution)/shard_map/ppermute | solution.py:12
  137.8 10.0 %collective-permute-start.2 = (bf16[256,768]{1,0:T(8,128)(2,1)S(1)}, bf16[256,768]{1,0:T(8,128)(2,1)S(1)}, u32[]{:S(2)}, u32[]{:S(2)}) collective-permute-start(bf16[256,768]{1,0:T(8,128)(2,1)S(1)} %collective-permute-done.1), channel_id=1, source_target_pairs={{0,8},{8,16},{16,24},{24,0},{1,9},{9,17},{17,25},{25,1},{2,10},{10... | collective-permute-start | bytes 1179656 | tf_op jit(solution)/shard_map/ppermute | solution.py:12
  150.0 1.0 copy-start.2
Sparse Core Ops, SparseCore 0:
  9.7 54.3 all-gather.3
  66.5 29.7 all-gather.5
  115.3 135.6 reduce-scatter.3
where the time goes:
time: 258 us
  waiting for transfers between devices  198 us (77%)
  matrix products  16.6 us (6%)
  between operations  15.1 us (6%)
  local copies, waits for them, and re-layouts  10.2 us (4%)
  blocking collectives  10.1 us (4%)
  other arithmetic  5.28 us (2%)
    unnamed x4, waiting for transfers between devices  99.2 us
    all_gather x1, waiting for transfers between devices, body(): lax.all_gather(linear_map_matrix, 'group', axis=0, tiled=True)  41.1 us
    ppermute x3, waiting for transfers between devices, passed_along(): return lax.ppermute(value, axis, pairs)  29.5 us
    all_gather x1, waiting for transfers between devices, body(): image_piece = lax.all_gather(image_unit, 'blk', axis=0, tiled=True)  28.3 us
    unnamed x9, local copies, waits for them, and re-layouts  10.2 us
    all_gather x1, blocking collectives, body(): label_piece = lax.all_gather(label_rows, 'blk', axis=0, tiled=True)  10.1 us
    dot_general x1, matrix products, body(): lax.dot_general(columns, projection_output_gradient, (((0,), (0,)), ((),...  5.27 us
  transfers between devices with their start and end apart: 6, of which 6 were waited for; matrix products, arithmetic and copies ran while one was open for 5% of the time, Pallas kernels for 0%

commit v1 on v0

--- a/solution.py
+++ b/solution.py
@@ -4,6 +4,30 @@
 from jax.sharding import PartitionSpec as P
 
 epsilon = 1e-06
+
+
+def compute_orders_here(q_in, in_dim):
+    known = list(q_in.shape[1:])
+    known[in_dim] *= q_in.shape[0]
+    return jnp.moveaxis(q_in, 0, in_dim).reshape(known)
+
+
+def step_on_signs(dimension_no, along_axis, vals):
+    full_n = lax.axis_size(along_axis)
+    items = tuple(((it, (it + 1) % full_n) for it in range(full_n)))
+    column = tuple(((dev, hop_no) for hop_no, dev in items))
+    front, tall = ([], [])
+    for tick in range(full_n - 1):
+        if tick % 2 == 0:
+            z = lax.ppermute(front[-1] if front else vals, along_axis, items)
+            front.append(z)
+        else:
+            tall.append(lax.ppermute(tall[-1] if tall else vals, along_axis, column))
+    frame_out = jnp.stack([*front[::-1], vals, *tall])
+    p_next = lax.axis_index(along_axis)
+    lower = p_next - len(front)
+    frame_out = frame_out[(jnp.arange(full_n) - lower) % full_n]
+    return compute_orders_here(frame_out, dimension_no)
 
 
 def passed_along(value, axis, steps):
@@ -31,9 +55,7 @@
     offset_value = offset_term[0]
     columns = hidden_rows
     projected = jnp.dot(
-        columns,
-        lax.all_gather(linear_map_matrix, "group", axis=0, tiled=True),
-        preferred_element_type=jnp.float32,
+        columns, step_on_signs(0, "group", linear_map_matrix), preferred_element_type=jnp.float32
     )
     text_scale = lax.rsqrt(jnp.sum(projected * projected, axis=1, keepdims=True) + epsilon)
     text_dir = projected * text_scale

time: 258 us -> 250 us (0.969)
  waiting for transfers between devices: 198 us -> 166 us
  local copies, waits for them, and re-layouts: 10.2 us -> 26.1 us
  starting transfers between devices: 2.2 us -> 11.6 us
    all_gather x1 -> x0, waiting for transfers between devices: 41.1 us -> none  [body(): lax.all_gather(linear_map_matrix, 'group', axis=0, tiled=True)]
    ppermute x0 -> x7, waiting for transfers between devices: none -> 37.6 us  [the longest x4 37.6 us: step_on_signs(): z = lax.ppermute(front[-1] if front else vals, along_axis, items)]
    all_gather x1, waiting for transfers between devices: 28.3 us -> 0.02 us  [body(): image_piece = lax.all_gather(image_unit, 'blk', axis=0, tiled=True)]
    unnamed x9 -> x18, local copies, waits for them, and re-layouts: 10.2 us -> 20 us
    ppermute x0 -> x7, starting transfers between devices: none -> 9.5 us  [the longest x3 8.99 us: step_on_signs(): tall.append(lax.ppermute(tall[-1] if tall else vals, along_axis, column))]
    gather x0 -> x1, local copies, waits for them, and re-layouts: none -> 5.35 us  [step_on_signs(): frame_out = frame_out[(jnp.arange(full_n) - lower) % full_n]]
    unnamed x4 -> x3, waiting for transfers between devices: 99.2 us -> 98.9 us
  transfers between devices with their start and end apart: 6 -> 12, of which waited for: 6 -> 7; matrix products, arithmetic and copies ran while one was open for 5% -> 12% of each run, Pallas kernels for 0% -> 0%
where the time goes in v1:
time: 250 us; the launch traced here: 249 us
  waiting for transfers between devices  166 us (66%)
  local copies, waits for them, and re-layouts  26.1 us (10%)
  matrix products  16.5 us (7%)
  between operations  15.5 us (6%)
  starting transfers between devices  11.6 us (5%)
  blocking collectives  8.28 us (3%)
  other arithmetic  5.25 us (2%)
    unnamed x3, waiting for transfers between devices  98.9 us
    ppermute x4, waiting for transfers between devices, step_on_signs(): z = lax.ppermute(front[-1] if front else vals, along_axis, items)  37.6 us
    ppermute x3, waiting for transfers between devices, passed_along(): return lax.ppermute(value, axis, pairs)  29.4 us
    unnamed x18, local copies, waits for them, and re-layouts  20 us
    ppermute x3, starting transfers between devices, step_on_signs(): tall.append(lax.ppermute(tall[-1] if tall else vals, along_axis, column))  8.99 us
    all_gather x1, blocking collectives, body(): label_piece = lax.all_gather(label_rows, 'blk', axis=0, tiled=True)  8.28 us
    gather x1, local copies, waits for them, and re-layouts, step_on_signs(): frame_out = frame_out[(jnp.arange(full_n) - lower) % full_n]  5.35 us
    dot_general x1, matrix products, body(): lax.dot_general(columns, projection_output_gradient, (((0,), (0,)), ((),...  5.09 us
  transfers between devices with their start and end apart: 12, of which 7 were waited for; matrix products, arithmetic and copies ran while one was open for 12% of the time, Pallas kernels for 0%

profile of v1, /device:TPU:0, one launch (start us, length us, event | category | flops | bytes accessed | tf_op | source)
XLA Modules:
  0.0 249.2 jit_solution(14052421555127993131)
XLA Ops:
  7.7 11.8 %collective-permute-done = bf16[384,768]{1,0:T(8,128)(2,1)S(1)} collective-permute-done((bf16[384,768]{1,0:T(8,128)(2,1)}, bf16[384,768]{1,0:T(8,128)(2,1)S(1)}, u32[]{:S(2)}, u32[]{:S(2)}) %collective-permute-start) | collective-permute-done | bytes 589856 | tf_op jit(solution)/shard_map/ppermute | solution.py:22
  19.6 3.5 %collective-permute-start.4 = (bf16[384,768]{1,0:T(8,128)(2,1)}, bf16[384,768]{1,0:T(8,128)(2,1)S(1)}, u32[]{:S(2)}, u32[]{:S(2)}) collective-permute-start(bf16[384,768]{1,0:T(8,128)(2,1)} %param.8), channel_id=1, source_target_pairs={{1,0},{2,1},{3,2},{4,3},{5,4},{6,5},{7,6},{0,7},{9,8},{10,9},{11,1... | collective-permute-start | bytes 1769480 | tf_op jit(solution)/shard_map/ppermute | solution.py:25
  23.1 13.1 %collective-permute-done.1 = bf16[384,768]{1,0:T(8,128)(2,1)} collective-permute-done((bf16[384,768]{1,0:T(8,128)(2,1)S(1)}, bf16[384,768]{1,0:T(8,128)(2,1)}, u32[]{:S(2)}, u32[]{:S(2)}) %collective-permute-start.1) | collective-permute-done | bytes 589856 | tf_op jit(solution)/shard_map/ppermute | solution.py:22
  36.2 1.2 fusion.27
  37.3 3.6 %collective-permute-start.5 = (bf16[384,768]{1,0:T(8,128)(2,1)S(1)}, bf16[384,768]{1,0:T(8,128)(2,1)}, u32[]{:S(2)}, u32[]{:S(2)}) collective-permute-start(bf16[384,768]{1,0:T(8,128)(2,1)S(1)} %collective-permute-done.4), channel_id=1, source_target_pairs={{1,0},{2,1},{3,2},{4,3},{5,4},{6,5},{7,6},{0,7},{9,8},{10,9},{11,1... | collective-permute-start | bytes 1769480 | tf_op jit(solution)/shard_map/ppermute | solution.py:25
  40.9 12.7 %collective-permute-done.2 = bf16[384,768]{1,0:T(8,128)(2,1)} collective-permute-done((bf16[384,768]{1,0:T(8,128)(2,1)}, bf16[384,768]{1,0:T(8,128)(2,1)}, u32[]{:S(2)}, u32[]{:S(2)}) %collective-permute-start.2) | collective-permute-done | bytes 589856 | tf_op jit(solution)/shard_map/ppermute | solution.py:22
  53.6 1.9 fusion.22
  56.9 8.3 %all-gather = s32[1,1024]{1,0:T(1,128)S(1)} all-gather(s32[1,256]{1,0:T(1,128)} %param.9), channel_id=2, replica_groups=mesh['blk'=4,'group'=8] {'blk'}, dimensions={1}, use_global_device_ids=true | all-gather | bytes 5120 | tf_op jit(solution)/shard_map/all_gather | solution.py:101
  65.7 1.9 collective-permute-start.6
  67.6 1.9 bitcast_dynamic-update-slice_fusion.7
  69.5 1.9 bitcast_dynamic-update-slice_fusion.6
  71.4 1.9 bitcast_dynamic-update-slice_fusion.5
  76.0 1.9 bitcast_dynamic-update-slice_fusion.1
  78.8 5.3 %gather_fusion = bf16[8,384,768]{2,1,0:T(8,128)(2,1)} fusion(bf16[8,384,768]{2,1,0:T(8,128)(2,1)} %bitcast_dynamic-update-slice_fusion, s32[1024]{0:T(1024)S(1)} %pad_clamp_fusion), kind=kCustom, calls=%fused_computation | custom fusion | bytes 9437216 | tf_op jit(solution)/shard_map/gather | solution.py:29
  84.1 3.8 %multiply_reduce_fusion = (f32[256]{0:T(256)S(1)}, f32[768,256]{1,0:T(8,128)S(1)}) fusion(bf16[3072,768]{1,0:T(8,128)(2,1)} %bitcast.85, bf16[1,256,3072]{2,1,0:T(8,128)(2,1)S(1)} %copy-done), kind=kOutput, calls=%fused_computation.47 | convolution fusion | flops 1208352512 | bytes 7078912 | tf_op jit(solution)/shard_map/dot_general | solution.py:57
  88.0 3.8 %fusion.28 = (f32[256]{0:T(256)S(1)}, f32[256,768]{0,1:T(8,128)S(1)}) fusion(f32[768,256]{1,0:T(8,128)S(1)} %get-tuple-element.14, f32[256]{0:T(256)S(1)} %add_rsqrt_fusion, bf16[1024,768]{1,0:T(8,128)(2,1)} %all-gather.3.cloned.1.call-done, bf16[256,768]{0,1:T(8,128)(2,1)S(1)} %bitcast_convert_fusion, f32[]{:T(128)} %bitcast.81, f32[]{:T(128)} %bitcast.72, ...), kind=kOutput, calls=%fused_computation.43 | convolution fusion | flops 809041664 | bytes 3546120 | tf_op jit(solution)/shard_map/dot_general | solution.py:104
  91.8 5.1 %convolution_bitcast_fusion = f32[3072,768]{0,1:T(8,128)} fusion(bf16[1,256,3072]{2,1,0:T(8,128)(2,1)S(1)} %copy-done, f32[256,768]{0,1:T(8,128)S(1)} %get-tuple-element.19, f32[768,256]{1,0:T(8,128)S(1)} %get-tuple-element.14, f32[256]{0:T(256)S(1)} %get-tuple-element.18, f32[256]{0:T(256)S(1)} %add_rsqrt_fusion), kind=kOutput, calls=%fused_computation.1 | convolution fusion | flops 1208942592 | bytes 12584960 | tf_op jit(solution)/shard_map/dot_general | solution.py:120
  96.9 9.6 %copy.16 = f32[3072,768]{1,0:T(8,128)} copy(f32[3072,768]{0,1:T(8,128)} %convolution_bitcast_fusion) | data formatting | bytes 18874368
  106.5 1.5 collective-permute-start.7
  108.0 10.3 %collective-permute-done.7 = bf16[256,768]{0,1:T(8,128)(2,1)S(1)} collective-permute-done((bf16[256,768]{0,1:T(8,128)(2,1)S(1)}, bf16[256,768]{0,1:T(8,128)(2,1)S(1)}, u32[]{:S(2)}, u32[]{:S(2)}) %collective-permute-start.7) | collective-permute-done | bytes 393248 | tf_op jit(solution)/shard_map/ppermute | solution.py:36
  119.2 10.0 %collective-permute-done.8 = bf16[256,768]{0,1:T(8,128)(2,1)S(1)} collective-permute-done((bf16[256,768]{0,1:T(8,128)(2,1)S(1)}, bf16[256,768]{0,1:T(8,128)(2,1)S(1)}, u32[]{:S(2)}, u32[]{:S(2)}) %collective-permute-start.8) | collective-permute-done | bytes 393248 | tf_op jit(solution)/shard_map/ppermute | solution.py:36
  130.0 9.2 %collective-permute-done.9 = bf16[256,768]{0,1:T(8,128)(2,1)S(1)} collective-permute-done((bf16[256,768]{0,1:T(8,128)(2,1)S(1)}, bf16[256,768]{0,1:T(8,128)(2,1)S(1)}, u32[]{:S(2)}, u32[]{:S(2)}) %collective-permute-start.9) | collective-permute-done | bytes 393248 | tf_op jit(solution)/shard_map/ppermute | solution.py:36
  139.5 1.0 fusion.76
  143.5 98.9 %reduce-scatter.4.cloned.1.call-done = f32[96,768]{1,0:T(8,128)} async-done(((f32[3072,768]{1,0:T(8,128)}), f32[96,768]{1,0:T(8,128)}) %reduce-scatter.4.cloned.1.call-update) | async-done | bytes 294928
  (46 shorter events, 9.8 us)
Async XLA Ops:
  7.2 77.0 %copy-start = (bf16[1,256,3072]{2,1,0:T(8,128)(2,1)S(1)}, bf16[1,256,3072]{2,1,0:T(8,128)(2,1)}, u32[]{:S(2)}) copy-start(bf16[1,256,3072]{2,1,0:T(8,128)(2,1)} %param.7) | copy-start | bytes 4718596
  7.2 67.1 %copy-start.3 = (bf16[384,768]{1,0:T(8,128)(2,1)S(1)}, bf16[384,768]{1,0:T(8,128)(2,1)}, u32[]{:S(2)}) copy-start(bf16[384,768]{1,0:T(8,128)(2,1)} %param.8) | copy-start | bytes 1769476
  7.2 80.8 %all-gather.3.cloned.1.call-start = ((), (), s32[]{:S(2)}) async-start(), calls=%async_computation.1 | async-start | bytes 1966080 | tf_op jit(solution)/shard_map/all_gather | solution.py:100
  7.2 12.3 %collective-permute-start = (bf16[384,768]{1,0:T(8,128)(2,1)}, bf16[384,768]{1,0:T(8,128)(2,1)S(1)}, u32[]{:S(2)}, u32[]{:S(2)}) collective-permute-start(bf16[384,768]{1,0:T(8,128)(2,1)} %param.8), channel_id=1, source_target_pairs={{0,1},{1,2},{2,3},{3,4},{4,5},{5,6},{6,7},{7,0},{8,9},{9,10},{10,1... | collective-permute-start | bytes 1769480 | tf_op jit(solution)/shard_map/ppermute | solution.py:22
  19.6 16.6 %collective-permute-start.1 = (bf16[384,768]{1,0:T(8,128)(2,1)S(1)}, bf16[384,768]{1,0:T(8,128)(2,1)}, u32[]{:S(2)}, u32[]{:S(2)}) collective-permute-start(bf16[384,768]{1,0:T(8,128)(2,1)S(1)} %collective-permute-done), channel_id=1, source_target_pairs={{0,1},{1,2},{2,3},{3,4},{4,5},{5,6},{6,7},{7,0},{8,9},{9,10},{10,1... | collective-permute-start | bytes 1769480 | tf_op jit(solution)/shard_map/ppermute | solution.py:22
  19.6 17.8 %collective-permute-start.4 = (bf16[384,768]{1,0:T(8,128)(2,1)}, bf16[384,768]{1,0:T(8,128)(2,1)S(1)}, u32[]{:S(2)}, u32[]{:S(2)}) collective-permute-start(bf16[384,768]{1,0:T(8,128)(2,1)} %param.8), channel_id=1, source_target_pairs={{1,0},{2,1},{3,2},{4,3},{5,4},{6,5},{7,6},{0,7},{9,8},{10,9},{11,1... | collective-permute-start | bytes 1769480 | tf_op jit(solution)/shard_map/ppermute | solution.py:25
  36.2 17.4 %collective-permute-start.2 = (bf16[384,768]{1,0:T(8,128)(2,1)}, bf16[384,768]{1,0:T(8,128)(2,1)}, u32[]{:S(2)}, u32[]{:S(2)}) collective-permute-start(bf16[384,768]{1,0:T(8,128)(2,1)} %collective-permute-done.1), channel_id=1, source_target_pairs={{0,1},{1,2},{2,3},{3,4},{4,5},{5,6},{6,7},{7,0},{8,9},{9,10},{10,1... | collective-permute-start | bytes 1769480 | tf_op jit(solution)/shard_map/ppermute | solution.py:22
  37.3 28.4 %collective-permute-start.5 = (bf16[384,768]{1,0:T(8,128)(2,1)S(1)}, bf16[384,768]{1,0:T(8,128)(2,1)}, u32[]{:S(2)}, u32[]{:S(2)}) collective-permute-start(bf16[384,768]{1,0:T(8,128)(2,1)S(1)} %collective-permute-done.4), channel_id=1, source_target_pairs={{1,0},{2,1},{3,2},{4,3},{5,4},{6,5},{7,6},{0,7},{9,8},{10,9},{11,1... | collective-permute-start | bytes 1769480 | tf_op jit(solution)/shard_map/ppermute | solution.py:25
  53.6 14.0 %collective-permute-start.3 = (bf16[384,768]{1,0:T(8,128)(2,1)}, bf16[384,768]{1,0:T(8,128)(2,1)}, u32[]{:S(2)}, u32[]{:S(2)}) collective-permute-start(bf16[384,768]{1,0:T(8,128)(2,1)} %collective-permute-done.2), channel_id=1, source_target_pairs={{0,1},{1,2},{2,3},{3,4},{4,5},{5,6},{6,7},{7,0},{8,9},{9,10},{10,1... | collective-permute-start | bytes 1769480 | tf_op jit(solution)/shard_map/ppermute | solution.py:22
  55.5 186.8 %reduce-scatter.4.cloned.1.call-start = ((), (), s32[]{:S(2)}) async-start(), calls=%async_computation.2 | async-start | bytes 9732096
  65.7 12.2 %collective-permute-start.6 = (bf16[384,768]{1,0:T(8,128)(2,1)}, bf16[384,768]{1,0:T(8,128)(2,1)S(1)}, u32[]{:S(2)}, u32[]{:S(2)}) collective-permute-start(bf16[384,768]{1,0:T(8,128)(2,1)} %collective-permute-done.5), channel_id=1, source_target_pairs={{1,0},{2,1},{3,2},{4,3},{5,4},{6,5},{7,6},{0,7},{9,8},{10,9},{11,1... | collective-permute-start | bytes 1769480 | tf_op jit(solution)/shard_map/ppermute | solution.py:25
  106.5 12.4 %copy-start.1 = (bf16[256,768]{1,0:T(8,128)(2,1)S(1)}, bf16[256,768]{1,0:T(8,128)(2,1)}, u32[]{:S(2)}) copy-start(bf16[256,768]{1,0:T(8,128)(2,1)} %fusion.22) | copy-start | bytes 1179652
  106.5 22.7 %copy-start.4 = (s32[1,256]{1,0:T(1,128)S(1)}, s32[1,256]{1,0:T(1,128)}, u32[]{:S(2)}) copy-start(s32[1,256]{1,0:T(1,128)} %param.9) | copy-start | bytes 3076
  106.5 11.8 %collective-permute-start.7 = (bf16[256,768]{0,1:T(8,128)(2,1)S(1)}, bf16[256,768]{0,1:T(8,128)(2,1)S(1)}, u32[]{:S(2)}, u32[]{:S(2)}) collective-permute-start(bf16[256,768]{0,1:T(8,128)(2,1)S(1)} %bitcast_convert_fusion), channel_id=1, source_target_pairs={{0,8},{8,16},{16,24},{24,0},{1,9},{9,17},{17,25},{25,1},{2,10},{10... | collective-permute-start | bytes 1179656 | tf_op jit(solution)/shard_map/ppermute | solution.py:36
  118.3 10.9 %collective-permute-start.8 = (bf16[256,768]{0,1:T(8,128)(2,1)S(1)}, bf16[256,768]{0,1:T(8,128)(2,1)S(1)}, u32[]{:S(2)}, u32[]{:S(2)}) collective-permute-start(bf16[256,768]{0,1:T(8,128)(2,1)S(1)} %collective-permute-done.7), channel_id=1, source_target_pairs={{0,8},{8,16},{16,24},{24,0},{1,9},{9,17},{17,25},{25,1},{2,10},{10... | collective-permute-start | bytes 1179656 | tf_op jit(solution)/shard_map/ppermute | solution.py:36
  129.2 9.9 %collective-permute-start.9 = (bf16[256,768]{0,1:T(8,128)(2,1)S(1)}, bf16[256,768]{0,1:T(8,128)(2,1)S(1)}, u32[]{:S(2)}, u32[]{:S(2)}) collective-permute-start(bf16[256,768]{0,1:T(8,128)(2,1)S(1)} %collective-permute-done.8), channel_id=1, source_target_pairs={{0,8},{8,16},{16,24},{24,0},{1,9},{9,17},{17,25},{25,1},{2,10},{10... | collective-permute-start | bytes 1179656 | tf_op jit(solution)/shard_map/ppermute | solution.py:36
  139.5 2.5 copy-start.2
Sparse Core Ops, SparseCore 0:
  55.6 32.3 all-gather.2
  106.7 135.6 reduce-scatter.3
